TPU v7x, 32 devices: a whole 2x2x4 slice. The times are simulated.
32 devices in a mesh: wave: 4 (over y, core), lev: 4 (over z), cpl: 2 (over x).
Axes of the slice: x: 2, y: 2, z: 4, core: 2. Of those that a mesh axis runs over, the one named last changes fastest.
Arguments:
- spectral: bfloat16 [1280, 2, 4, 24, 1280], P('wave', None, None, 'lev'), may hold values from -0.125 to 0.125
- legendre: bfloat16 [1280, 16, 1280], P('wave', 'cpl'), may hold values from -0.15625 to 0.15625
- wavenumber: int32 [1280], replicated, may hold values from 0 to 1279, each once
- level_weight: float32 [24], P('lev'), may hold values from 0.1 to 1
- source_row: int32 [16], replicated, may hold values from 0 to 14
- row_weight: float32 [16], replicated, may hold values from 0.2 to 0.8
Outputs:
- ocean_flux: float32 [16, 4, 4320], P(('wave', 'cpl'), None, 'lev')
All inputs are finite; a program needn't handle non-finite values.
Results may differ from a plain program's by a relative error of at most 0.0041.
Values may be sent and summed in bfloat16 or wider, within the bound.
No kernel may reach another device: no remote copies, remote signals or barrier semaphores. Data moves between devices by JAX's collectives and lax.ppermute only.
A program may use at most 192 MiB of HBM per device.

v0:
```python
import math
import jax
import jax.numpy as jnp
from jax import lax
from jax.sharding import PartitionSpec as P

NLON = 4320
LANE = 128


def phase_angle(phase, lon_total):
    return phase.astype(jnp.float32) * (2.0 * math.pi / lon_total)


def surface_flux(grid_vals, level_weight):
    wind_speed = jnp.sqrt(grid_vals[:, 0] ** 2 + grid_vals[:, 1] ** 2 + 0.25)
    return jnp.sum(level_weight[:, None] * wind_speed[:, None] * grid_vals, axis=2)


def latitude_order(gathered, wave_count, cpl_count, lat_dev):
    trailing = gathered.shape[1:]
    gathered = gathered.reshape((wave_count, cpl_count, lat_dev) + trailing)
    gathered = jnp.swapaxes(gathered, 0, 1)
    return gathered.reshape((wave_count * cpl_count * lat_dev,) + trailing)


def interpolate(gathered, source, weight_hi):
    lower = jnp.take(gathered, source, axis=0)
    upper = jnp.take(gathered, source + 1, axis=0)
    return (1.0 - weight_hi[:, None, None]) * lower + weight_hi[:, None, None] * upper


def quarter_tables(wavenumber, width):
    blocks = width // LANE
    factor = jnp.where(wavenumber == 0, 1.0, 2.0).astype(jnp.float32)[:, None]
    offsets = jnp.arange(LANE, dtype=jnp.int32)
    base_angle = phase_angle(wavenumber[:, None] * offsets[None, :] % NLON, NLON)
    base_cos = jnp.cos(base_angle)[:, None, :]
    base_sin = jnp.sin(base_angle)[:, None, :]
    starts = jnp.arange(blocks, dtype=jnp.int32) * LANE
    start_angle = phase_angle(wavenumber[:, None] * starts[None, :] % NLON, NLON)
    start_cos = (factor * jnp.cos(start_angle))[:, :, None]
    start_sin = (factor * jnp.sin(start_angle))[:, :, None]
    cos_tab = start_cos * base_cos - start_sin * base_sin
    sin_tab = start_sin * base_cos + start_cos * base_sin
    slots = wavenumber.shape[0]
    return (
        cos_tab.astype(jnp.bfloat16).reshape(slots, width),
        (-sin_tab).astype(jnp.bfloat16).reshape(slots, width),
    )


def local(spectral, legendre, wavenumber, level_weight, source_row, row_weight):
    slot_count = spectral.shape[0]
    fields = spectral.shape[2]
    levels = spectral.shape[3]
    degree = spectral.shape[4]
    channels = 2 * fields * levels
    wave_count = lax.axis_size("wave")
    cpl_count = lax.axis_size("cpl")
    lev_count = lax.axis_size("lev")
    wave_at = lax.axis_index("wave")
    cpl_at = lax.axis_index("cpl")
    owned_waves = lax.dynamic_slice_in_dim(wavenumber, wave_at * slot_count, slot_count)
    in_triangle = (
        lax.broadcasted_iota(jnp.int32, (slot_count, 1, degree), 2)
        < (degree - owned_waves)[:, None, None]
    )
    table_rows = jnp.where(in_triangle, legendre, jnp.zeros_like(legendre))
    coefficient = spectral.reshape(slot_count, channels, degree)
    spec_grid = jnp.einsum(
        "skj,slj->slk", coefficient, table_rows, preferred_element_type=jnp.float32
    ).astype(jnp.bfloat16)
    by_latitude = lax.all_to_all(spec_grid, "wave", split_axis=1, concat_axis=0, tiled=True)
    total_slots = by_latitude.shape[0]
    lat_dev = by_latitude.shape[1]
    rows = lat_dev * fields * levels
    parts = by_latitude.reshape(total_slots, lat_dev, 2, fields * levels)
    real = parts[:, :, 0].reshape(total_slots, rows).T
    imag = parts[:, :, 1].reshape(total_slots, rows).T
    parity = (1 - 2 * (wavenumber & 1)).astype(jnp.bfloat16)[None, :]
    lhs_cos = jnp.concatenate([real, real * parity], axis=0)
    lhs_sin = jnp.concatenate([imag, imag * parity], axis=0)
    quarter = NLON // 4
    width = -(-(quarter + 1) // LANE) * LANE
    cos_tab, sin_tab = quarter_tables(wavenumber, width)
    r_all = jnp.dot(lhs_cos, cos_tab, preferred_element_type=jnp.float32)
    q_all = jnp.dot(lhs_sin, sin_tab, preferred_element_type=jnp.float32)
    r1, r2 = (r_all[:rows], r_all[rows:])
    q1, q2 = (q_all[:rows], q_all[rows:])

    def flux_of(grid_rows):
        return surface_flux(grid_rows.reshape(lat_dev, fields, levels, quarter), level_weight)

    strip0 = flux_of((r1 + q1)[:, :quarter])
    strip1 = jnp.flip(flux_of((r2 - q2)[:, 1 : quarter + 1]), axis=-1)
    strip2 = flux_of((r2 + q2)[:, :quarter])
    strip3 = jnp.flip(flux_of((r1 - q1)[:, 1 : quarter + 1]), axis=-1)
    partial_value = jnp.concatenate([strip0, strip1, strip2, strip3], axis=-1)
    own_first = (wave_at * cpl_count + cpl_at) * lat_dev
    source = lax.dynamic_slice_in_dim(source_row, own_first, lat_dev)
    weight_hi = lax.dynamic_slice_in_dim(row_weight, own_first, lat_dev)
    strip_width = NLON // lev_count
    by_strip = partial_value.reshape(lat_dev, fields, lev_count, strip_width).transpose(2, 0, 1, 3)
    summed = jnp.sum(
        lax.all_to_all(by_strip, "lev", split_axis=0, concat_axis=0, tiled=True), axis=0
    )
    copies = jnp.broadcast_to(summed[None], (wave_count * cpl_count,) + summed.shape)
    gathered = lax.all_to_all(copies, ("wave", "cpl"), split_axis=0, concat_axis=0, tiled=True)
    gathered = gathered.reshape((wave_count * cpl_count * lat_dev,) + summed.shape[1:])
    gathered = latitude_order(gathered, wave_count, cpl_count, lat_dev)
    return interpolate(gathered, source, weight_hi)


def solution(mesh):
    placed = (P("wave", None, None, "lev", None), P("wave", "cpl", None), P(), P("lev"), P(), P())
    return jax.shard_map(
        local,
        mesh=mesh,
        in_specs=placed,
        out_specs=P(("wave", "cpl"), None, "lev"),
        check_vma=False,
    )
```

profile of v0, /device:TPU:0, one launch (start us, length us, event | category | flops | bytes accessed | tf_op | source)
XLA Modules:
  0.0 121.1 jit_solution(9876910115910982764)
XLA Ops:
  0.0 0.8 dynamic-slice_subtract_fusion
  0.8 0.3 iota_compare_fusion
  1.1 26.6 %copy.19 = bf16[320,2,4,6,1280]{4,0,3,2,1:T(8,128)(2,1)} copy(bf16[320,2,4,6,1280]{4,2,3,1,0:T(4,128)(2,1)} %param.8) | data formatting | bytes 78643200 | tf_op args[0]
  27.7 0.0 copy-start
  27.7 47.5 %fusion.5 = bf16[320,8,48]{2,1,0:T(8,128)(2,1)S(1)} fusion(bf16[320,48,1280]{2,0,1:T(8,128)(2,1)} %bitcast.34, bf16[320,8,1280]{2,1,0:T(8,128)(2,1)} %param.9, pred[320,1280]{1,0:T(8,128)(4,1)S(1)} %iota_compare_fusion), kind=kOutput, calls=%fused_computation.10 | convolution fusion | flops 317972480 | bytes 46530560 | tf_op jit(solution)/shard_map/skj,slj->slk/dot_general | solution.py:71
  75.2 1.1 copy.21
  76.4 4.2 %all-to-all-start = ((bf16[320,8,48]{0,2,1:T(8,128)(2,1)}), bf16[320,8,48]{0,2,1:T(8,128)(2,1)S(1)}, u32[]{:S(2)}, u32[]{:S(2)}) async-start(bf16[320,8,48]{0,2,1:T(8,128)(2,1)} %copy.21), calls=%async_computation | async-start | bytes 589824 | tf_op jit(solution)/shard_map/all_to_all | solution.py:74
  80.6 0.0 copy-done
  80.6 2.6 %fusion.15 = (f32[1280,128]{0,1:T(8,128)S(1)}, f32[1280,128]{0,1:T(8,128)S(1)}) fusion(s32[1280]{0:T(1024)S(1)} %copy-done), kind=kLoop, calls=%fused_computation.18 | loop fusion | flops 1474560 | bytes 1315840 | tf_op jit(solution)/shard_map/cos | solution.py:38
  83.3 0.4 cosine_multiply_fusion
  83.7 3.3 %subtract_convert_fusion = (bf16[1280,9,128]{0,2,1:T(8,128)(2,1)}, bf16[1280,9,128]{0,2,1:T(8,128)(2,1)S(1)}) fusion(f32[1280,128]{0,1:T(8,128)S(1)} %get-tuple-element.27, f32[1280,9]{0,1:T(8,128)S(1)} %get-tuple-element.25, f32[1280,128]{0,1:T(8,128)S(1)} %get-tuple-element.26, f32[1280,9]{0,1:T(8,128)S(1)} %get-tuple-element.24), kind=kLoop, calls=%fused_computation.7 | loop fusion | flops 13271040 | bytes 7301120 | tf_op jit(solution)/shard_map/convert_element_type | solution.py:48
  87.0 0.0 all-to-all-done
  87.0 0.2 copy.30
  87.2 0.3 reshape.215
  87.5 2.8 %fusion.17 = f32[96,1152]{1,0:T(8,128)S(1)} fusion(bf16[1280,1152]{0,1:T(8,128)(2,1)} %bitcast.36, bf16[48,1280]{1,0:T(8,128)(2,1)S(1)} %get-tuple-element.28, bf16[48,1280]{1,0:T(8,128)(2,1)S(1)} %bitcast.41), kind=kOutput, calls=%fused_computation.25 | convolution fusion | flops 283607040 | bytes 3637248 | tf_op jit(solution)/shard_map/dot_general | solution.py:87
  90.4 0.0 copy-start.1
  90.4 1.0 fusion.21
  91.4 0.0 copy-start.2
  91.5 0.0 copy-start.3
  91.5 0.3 slice_subtract_fusion
  92.0 0.0 copy-done.1
  92.0 0.2 fusion.34
  92.2 0.1 multiply_reduce_fusion
  92.3 0.8 reverse.1
  93.1 0.1 slice.163
  93.2 0.1 multiply_reduce_fusion.1
  93.3 0.1 multiply_reduce_fusion.2
  93.4 0.8 reverse
  94.2 0.1 slice.162
  94.3 0.1 multiply_reduce_fusion.3
  94.4 0.2 concatenate.11
  94.6 0.2 reshape.220
  94.8 0.7 copy.23
  95.5 5.5 %all-to-all-start.1 = ((f32[4,2,4,1080]{3,2,1,0:T(4,128)}), f32[4,2,4,1080]{3,2,1,0:T(4,128)S(1)}, u32[]{:S(2)}, u32[]{:S(2)}) async-start(f32[4,2,4,1080]{3,2,1,0:T(4,128)} %copy.23), calls=%async_computation.1 | async-start | bytes 294912 | tf_op jit(solution)/shard_map/all_to_all | solution.py:106
  101.0 6.6 %all-to-all-done.1 = f32[4,2,4,1080]{3,2,1,0:T(4,128)S(1)} async-done(((f32[4,2,4,1080]{3,2,1,0:T(4,128)}), f32[4,2,4,1080]{3,2,1,0:T(4,128)S(1)}, u32[]{:S(2)}, u32[]{:S(2)}) %all-to-all-start.1) | async-done | bytes 138272 | tf_op jit(solution)/shard_map/all_to_all | solution.py:106
  107.7 0.7 broadcast_in_dim.30
  108.5 4.0 %all-to-all-start.2 = ((f32[8,2,4,1080]{3,2,1,0:T(4,128)}), f32[8,2,4,1080]{3,2,1,0:T(4,128)S(1)}, u32[]{:S(2)}, u32[]{:S(2)}) async-start(f32[8,2,4,1080]{3,2,1,0:T(4,128)} %broadcast_in_dim.30), calls=%async_computation.2 | async-start | bytes 589824 | tf_op jit(solution)/shard_map/all_to_all | solution.py:109
  112.4 0.0 copy-done.2
  112.4 0.1 broadcast_subtract_fusion
  112.5 0.0 copy-done.3
  112.5 0.1 compare_and_fusion.1
  112.6 6.6 %all-to-all-done.2 = f32[8,2,4,1080]{3,2,1,0:T(4,128)S(1)} async-done(((f32[8,2,4,1080]{3,2,1,0:T(4,128)}), f32[8,2,4,1080]{3,2,1,0:T(4,128)S(1)}, u32[]{:S(2)}, u32[]{:S(2)}) %all-to-all-start.2) | async-done | bytes 276512 | tf_op jit(solution)/shard_map/all_to_all | solution.py:109
  119.3 0.6 gather_fusion
  119.9 0.6 gather_fusion.1
  120.4 0.7 fusion.50
  (14 shorter events, 0.3 us)
Async XLA Ops:
  27.7 52.9 %copy-start = (s32[1280]{0:T(1024)S(1)}, s32[1280]{0:T(1024)}, u32[]{:S(2)}) copy-start(s32[1280]{0:T(1024)} %param.10) | copy-start | bytes 15364
  76.4 10.7 %all-to-all-start = ((bf16[320,8,48]{0,2,1:T(8,128)(2,1)}), bf16[320,8,48]{0,2,1:T(8,128)(2,1)S(1)}, u32[]{:S(2)}, u32[]{:S(2)}) async-start(bf16[320,8,48]{0,2,1:T(8,128)(2,1)} %copy.21), calls=%async_computation | async-start | bytes 589824 | tf_op jit(solution)/shard_map/all_to_all | solution.py:74
  90.4 1.6 %copy-start.1 = (f32[6]{0:T(128)S(1)}, f32[6]{0:T(128)}, u32[]{:S(2)}) copy-start(f32[6]{0:T(128)} %param.11) | copy-start | bytes 76
  91.4 21.0 %copy-start.2 = (f32[16]{0:T(128)S(1)}, f32[16]{0:T(128)}, u32[]{:S(2)}) copy-start(f32[16]{0:T(128)} %param.13) | copy-start | bytes 196
  91.5 21.1 %copy-start.3 = (s32[16]{0:T(128)S(1)}, s32[16]{0:T(128)}, u32[]{:S(2)}) copy-start(s32[16]{0:T(128)} %param.12) | copy-start | bytes 196
  95.5 12.2 %all-to-all-start.1 = ((f32[4,2,4,1080]{3,2,1,0:T(4,128)}), f32[4,2,4,1080]{3,2,1,0:T(4,128)S(1)}, u32[]{:S(2)}, u32[]{:S(2)}) async-start(f32[4,2,4,1080]{3,2,1,0:T(4,128)} %copy.23), calls=%async_computation.1 | async-start | bytes 294912 | tf_op jit(solution)/shard_map/all_to_all | solution.py:106
  108.5 10.8 %all-to-all-start.2 = ((f32[8,2,4,1080]{3,2,1,0:T(4,128)}), f32[8,2,4,1080]{3,2,1,0:T(4,128)S(1)}, u32[]{:S(2)}, u32[]{:S(2)}) async-start(f32[8,2,4,1080]{3,2,1,0:T(4,128)} %broadcast_in_dim.30), calls=%async_computation.2 | async-start | bytes 589824 | tf_op jit(solution)/shard_map/all_to_all | solution.py:109
where the time goes:
time: 122 us; the launch traced here: 121 us
  matrix products  51.4 us (42%)
  local copies, waits for them, and re-layouts  33.2 us (27%)
  starting transfers between devices  13.8 us (11%)
  waiting for transfers between devices  13.3 us (11%)
  other arithmetic  9.35 us (8%)
    dot_general x1, matrix products, local(): jnp.einsum('skj,slj->slk', coefficient, table_rows, preferred_element_typ...  47.5 us
    unnamed x13, local copies, waits for them, and re-layouts  28.4 us
    all_to_all x1, waiting for transfers between devices, local(): lax.all_to_all(by_strip, 'lev', split_axis=0, concat_axis=0, tiled=True)  6.64 us
    all_to_all x1, waiting for transfers between devices, local(): lax.all_to_all(copies, ('wave', 'cpl'), split_axis=0, concat_axis=0, tile...  6.63 us
    all_to_all x1, starting transfers between devices, local(): lax.all_to_all(by_strip, 'lev', split_axis=0, concat_axis=0, tiled=True)  5.55 us
    all_to_all x1, starting transfers between devices, local(): lax.all_to_all(spec_grid, 'wave', split_axis=1, concat_axis=0, tiled=True)  4.24 us
    all_to_all x1, starting transfers between devices, local(): lax.all_to_all(copies, ('wave', 'cpl'), split_axis=0, concat_axis=0, tile...  3.98 us
    convert_element_type x1, other arithmetic, quarter_tables(): cos_tab.astype(jnp.bfloat16).reshape(slots, width)  3.34 us
  transfers between devices with their start and end apart: 3, of which 2 were waited for; matrix products, arithmetic and copies ran while one was open for 5% of the time, Pallas kernels for 0%

commit v1 on v0

--- a/solution.py
+++ b/solution.py
@@ -71,7 +71,9 @@
     spec_grid = jnp.einsum(
         "skj,slj->slk", coefficient, table_rows, preferred_element_type=jnp.float32
     ).astype(jnp.bfloat16)
-    by_latitude = lax.all_to_all(spec_grid, "wave", split_axis=1, concat_axis=0, tiled=True)
+    pieces = jnp.split(spec_grid, lax.axis_size("wave"), axis=1)
+    got = lax.all_to_all(jnp.stack(pieces), "wave", 0, 0)
+    by_latitude = jnp.concatenate(got, axis=0)
     total_slots = by_latitude.shape[0]
     lat_dev = by_latitude.shape[1]
     rows = lat_dev * fields * levels

time: 122 us -> 122 us (level)
    another operation x0 -> x6, local copies, waits for them, and re-layouts: none -> 1.27 us  [the longest x5 1.01 us: local(): got = lax.all_to_all(jnp.stack(pieces), 'wave', 0, 0)]
where the time goes in v1:
time: 122 us
  matrix products  51.3 us (42%)
  local copies, waits for them, and re-layouts  33.1 us (27%)
  starting transfers between devices  13.8 us (11%)
  waiting for transfers between devices  13.3 us (11%)
  other arithmetic  10.2 us (8%)
    dot_general x1, matrix products, local(): jnp.einsum('skj,slj->slk', coefficient, table_rows, preferred_element_typ...  47.4 us
    unnamed x13, local copies, waits for them, and re-layouts  28.5 us
    all_to_all x1, waiting for transfers between devices, local(): lax.all_to_all(by_strip, 'lev', split_axis=0, concat_axis=0, tiled=True)  6.64 us
    all_to_all x1, waiting for transfers between devices, local(): lax.all_to_all(copies, ('wave', 'cpl'), split_axis=0, concat_axis=0, tile...  6.63 us
    all_to_all x1, starting transfers between devices, local(): lax.all_to_all(by_strip, 'lev', split_axis=0, concat_axis=0, tiled=True)  5.55 us
    all_to_all x1, starting transfers between devices, local(): got = lax.all_to_all(jnp.stack(pieces), 'wave', 0, 0)  4.24 us
    all_to_all x1, starting transfers between devices, local(): lax.all_to_all(copies, ('wave', 'cpl'), split_axis=0, concat_axis=0, tile...  3.98 us
    convert_element_type x1, other arithmetic, quarter_tables(): cos_tab.astype(jnp.bfloat16).reshape(slots, width)  3.34 us
  transfers between devices with their start and end apart: 3, of which 2 were waited for; matrix products, arithmetic and copies ran while one was open for 5% of the time, Pallas kernels for 0%

profile of v1, /device:TPU:0, one launch (start us, length us, event | category | flops | bytes accessed | tf_op | source)
XLA Modules:
  0.0 121.8 jit_solution(18119571799722693849)
XLA Ops:
  0.0 0.8 dynamic-slice_subtract_fusion
  0.8 0.3 iota_compare_fusion
  1.1 26.6 %copy.22 = bf16[320,2,4,6,1280]{4,0,3,2,1:T(8,128)(2,1)} copy(bf16[320,2,4,6,1280]{4,2,3,1,0:T(4,128)(2,1)} %param.8) | data formatting | bytes 78643200 | tf_op args[0]
  27.7 0.0 copy-start
  27.7 47.4 %fusion.5 = bf16[320,8,48]{2,1,0:T(8,128)(2,1)S(1)} fusion(bf16[320,48,1280]{2,0,1:T(8,128)(2,1)} %bitcast.38, bf16[320,8,1280]{2,1,0:T(8,128)(2,1)} %param.9, pred[320,1280]{1,0:T(8,128)(4,1)S(1)} %iota_compare_fusion), kind=kOutput, calls=%fused_computation.10 | convolution fusion | flops 317972480 | bytes 46530560 | tf_op jit(solution)/shard_map/skj,slj->slk/dot_general | solution.py:71
  75.2 0.5 slice_bitcast_fusion.3
  75.6 0.1 copy.24
  75.8 0.1 copy.25
  75.9 0.1 copy.26
  76.1 0.1 copy.27
  76.2 0.8 pad_maximum_fusion
  77.0 4.2 %all-to-all-start = ((bf16[4,320,2,48]{1,3,2,0:T(8,128)(2,1)}), bf16[4,320,2,48]{1,3,2,0:T(8,128)(2,1)S(1)}, u32[]{:S(2)}, u32[]{:S(2)}) async-start(bf16[4,320,2,48]{1,3,2,0:T(8,128)(2,1)} %pad_maximum_fusion), calls=%async_computation | async-start | bytes 589824 | tf_op jit(solution)/shard_map/all_to_all | solution.py:75
  81.2 0.0 copy-done
  81.3 2.6 %fusion.15 = (f32[1280,128]{0,1:T(8,128)S(1)}, f32[1280,128]{0,1:T(8,128)S(1)}) fusion(s32[1280]{0:T(1024)S(1)} %copy-done), kind=kLoop, calls=%fused_computation.18 | loop fusion | flops 1474560 | bytes 1315840 | tf_op jit(solution)/shard_map/cos | solution.py:38
  83.9 0.4 cosine_multiply_fusion
  84.3 3.3 %subtract_convert_fusion = (bf16[1280,9,128]{0,2,1:T(8,128)(2,1)}, bf16[1280,9,128]{0,2,1:T(8,128)(2,1)S(1)}) fusion(f32[1280,128]{0,1:T(8,128)S(1)} %get-tuple-element.31, f32[1280,9]{0,1:T(8,128)S(1)} %get-tuple-element.29, f32[1280,128]{0,1:T(8,128)S(1)} %get-tuple-element.30, f32[1280,9]{0,1:T(8,128)S(1)} %get-tuple-element.28), kind=kLoop, calls=%fused_computation.7 | loop fusion | flops 13271040 | bytes 7301120 | tf_op jit(solution)/shard_map/convert_element_type | solution.py:48
  87.7 0.0 all-to-all-done
  87.7 0.2 copy.28
  87.8 0.3 reshape_reshape.6
  88.2 2.8 %fusion.17 = f32[96,1152]{1,0:T(8,128)S(1)} fusion(bf16[1280,1152]{0,1:T(8,128)(2,1)} %bitcast.40, bf16[48,1280]{1,0:T(8,128)(2,1)S(1)} %get-tuple-element.32, bf16[48,1280]{1,0:T(8,128)(2,1)S(1)} %bitcast.43), kind=kOutput, calls=%fused_computation.25 | convolution fusion | flops 283607040 | bytes 3637248 | tf_op jit(solution)/shard_map/dot_general | solution.py:89
  91.0 0.0 copy-start.1
  91.1 1.0 fusion.21
  92.1 0.0 copy-start.2
  92.1 0.0 copy-start.3
  92.1 0.3 slice_subtract_fusion
  92.6 0.0 copy-done.1
  92.6 0.2 fusion.34
  92.8 0.1 multiply_reduce_fusion
  92.9 0.8 reverse.1
  93.7 0.1 slice.163
  93.8 0.1 multiply_reduce_fusion.1
  93.9 0.1 multiply_reduce_fusion.2
  94.1 0.8 reverse
  94.9 0.1 slice.162
  95.0 0.1 multiply_reduce_fusion.3
  95.1 0.2 concatenate.11
  95.3 0.2 reshape.215
  95.4 0.7 copy.29
  96.1 5.6 %all-to-all-start.1 = ((f32[4,2,4,1080]{3,2,1,0:T(4,128)}), f32[4,2,4,1080]{3,2,1,0:T(4,128)S(1)}, u32[]{:S(2)}, u32[]{:S(2)}) async-start(f32[4,2,4,1080]{3,2,1,0:T(4,128)} %copy.29), calls=%async_computation.1 | async-start | bytes 294912 | tf_op jit(solution)/shard_map/all_to_all | solution.py:108
  101.7 6.6 %all-to-all-done.1 = f32[4,2,4,1080]{3,2,1,0:T(4,128)S(1)} async-done(((f32[4,2,4,1080]{3,2,1,0:T(4,128)}), f32[4,2,4,1080]{3,2,1,0:T(4,128)S(1)}, u32[]{:S(2)}, u32[]{:S(2)}) %all-to-all-start.1) | async-done | bytes 138272 | tf_op jit(solution)/shard_map/all_to_all | solution.py:108
  108.4 0.8 broadcast_in_dim.30
  109.1 4.0 %all-to-all-start.2 = ((f32[8,2,4,1080]{3,2,1,0:T(4,128)}), f32[8,2,4,1080]{3,2,1,0:T(4,128)S(1)}, u32[]{:S(2)}, u32[]{:S(2)}) async-start(f32[8,2,4,1080]{3,2,1,0:T(4,128)} %broadcast_in_dim.30), calls=%async_computation.2 | async-start | bytes 589824 | tf_op jit(solution)/shard_map/all_to_all | solution.py:111
  113.1 0.0 copy-done.2
  113.1 0.1 broadcast_subtract_fusion
  113.2 0.0 copy-done.3
  113.2 0.1 compare_and_fusion.1
  113.3 6.6 %all-to-all-done.2 = f32[8,2,4,1080]{3,2,1,0:T(4,128)S(1)} async-done(((f32[8,2,4,1080]{3,2,1,0:T(4,128)}), f32[8,2,4,1080]{3,2,1,0:T(4,128)S(1)}, u32[]{:S(2)}, u32[]{:S(2)}) %all-to-all-start.2) | async-done | bytes 276512 | tf_op jit(solution)/shard_map/all_to_all | solution.py:111
  119.9 0.6 gather_fusion
  120.5 0.6 gather_fusion.1
  121.1 0.7 fusion.50
  (14 shorter events, 0.3 us)
Async XLA Ops:
  27.7 53.5 %copy-start = (s32[1280]{0:T(1024)S(1)}, s32[1280]{0:T(1024)}, u32[]{:S(2)}) copy-start(s32[1280]{0:T(1024)} %param.10) | copy-start | bytes 15364
  77.0 10.7 %all-to-all-start = ((bf16[4,320,2,48]{1,3,2,0:T(8,128)(2,1)}), bf16[4,320,2,48]{1,3,2,0:T(8,128)(2,1)S(1)}, u32[]{:S(2)}, u32[]{:S(2)}) async-start(bf16[4,320,2,48]{1,3,2,0:T(8,128)(2,1)} %pad_maximum_fusion), calls=%async_computation | async-start | bytes 589824 | tf_op jit(solution)/shard_map/all_to_all | solution.py:75
  91.0 1.6 %copy-start.1 = (f32[6]{0:T(128)S(1)}, f32[6]{0:T(128)}, u32[]{:S(2)}) copy-start(f32[6]{0:T(128)} %param.11) | copy-start | bytes 76
  92.1 21.0 %copy-start.2 = (f32[16]{0:T(128)S(1)}, f32[16]{0:T(128)}, u32[]{:S(2)}) copy-start(f32[16]{0:T(128)} %param.13) | copy-start | bytes 196
  92.1 21.1 %copy-start.3 = (s32[16]{0:T(128)S(1)}, s32[16]{0:T(128)}, u32[]{:S(2)}) copy-start(s32[16]{0:T(128)} %param.12) | copy-start | bytes 196
  96.1 12.2 %all-to-all-start.1 = ((f32[4,2,4,1080]{3,2,1,0:T(4,128)}), f32[4,2,4,1080]{3,2,1,0:T(4,128)S(1)}, u32[]{:S(2)}, u32[]{:S(2)}) async-start(f32[4,2,4,1080]{3,2,1,0:T(4,128)} %copy.29), calls=%async_computation.1 | async-start | bytes 294912 | tf_op jit(solution)/shard_map/all_to_all | solution.py:108
  109.1 10.8 %all-to-all-start.2 = ((f32[8,2,4,1080]{3,2,1,0:T(4,128)}), f32[8,2,4,1080]{3,2,1,0:T(4,128)S(1)}, u32[]{:S(2)}, u32[]{:S(2)}) async-start(f32[8,2,4,1080]{3,2,1,0:T(4,128)} %broadcast_in_dim.30), calls=%async_computation.2 | async-start | bytes 589824 | tf_op jit(solution)/shard_map/all_to_all | solution.py:111
